TPU v7x, 128 devices: a whole 4x4x4 slice. The times are simulated.
128 devices in a mesh: group: 16 (over x, z), mp: 8 (over y, core).
Axes of the slice: x: 4, y: 4, z: 4, core: 2. Of those that a mesh axis runs over, the one named last changes fastest.
Arguments:
- stream: bfloat16 [8192, 3584], P('group', 'mp'), may hold values from -6 to 6
- prenorm_gain: float32 [3584], replicated, may hold values from 0.25 to 12
- query_weight: bfloat16 [3584, 4096], P(None, 'mp'), may hold values from -0.09375 to 0.09375
- key_weight: bfloat16 [3584, 2048], P(None, 'mp'), may hold values from -0.09375 to 0.09375
- value_weight: bfloat16 [3584, 2048], P(None, 'mp'), may hold values from -0.09375 to 0.09375
- output_weight: bfloat16 [4096, 3584], P('mp'), may hold values from -0.09375 to 0.09375
- adapter_down_rows: bfloat16 [64, 16, 3584], P('group', None, 'mp'), may hold values from -0.09375 to 0.09375
- adapter_up_query: bfloat16 [64, 16, 4096], P('group', None, 'mp'), may hold values from -1.5 to 1.5
- request_adapter: int32 [16, 4], replicated, may hold values from 0 to 63
- adapter_row_index: int32 [64], replicated, may hold values from 0 to 63, each once
- request_token_length: int32 [16, 4], replicated, may hold values from 1 to 256, 512 in all within a row
- continues_previous: int32 [16], replicated, may hold values from 0 to 1, as said below
- request_cache_block: int32 [16, 4], replicated, may hold values from 0 to 31, as said below
- cached_length: int32 [16, 4], replicated, may hold values from 1 to 256
- cached_rotated_keys: bfloat16 [32, 256, 2048], P('group', None, 'mp'), may hold values from -6 to 6
- cached_value_rows: bfloat16 [32, 256, 2048], P('group', None, 'mp'), may hold values from -6 to 6
Outputs:
- attn_out: bfloat16 [8192, 3584], P('group', 'mp')
Inputs may be any that keep to these rules, and one draw needn't show every extreme that they name: `continues_previous`: the first group has 0; some group has 1. `request_cache_block`: the owner of block b is group b // 2; blocks may be shared by requests.
All inputs are finite; a program needn't handle non-finite values.
Results may differ from a plain program's by a relative error of at most 0.017.
The roundings to bfloat16 on the way count: a program that leaves them out, or rounds other values in their place, can miss the bound.
Values may be sent and summed in bfloat16 or wider, within the bound.
No kernel may reach another device: no remote copies, remote signals or barrier semaphores. Data moves between devices by JAX's collectives and lax.ppermute only.
A program may use at most 128 MiB of HBM per device.

v0:
```python
import jax
import jax.numpy as jnp
from jax import lax
from jax.sharding import PartitionSpec as P

HEAD_WIDTH = 256
REQS = 4
adapter_scale = 2.0


def shifted(value, axis, steps):
    count = lax.axis_size(axis)
    first, last = (max(0, -steps), min(count, count - steps))
    return lax.ppermute(value, axis, [(source, source + steps) for source in range(first, last)])


def rotate(values, position, head_size):
    count = values.shape[0]
    shaped = values.reshape(count, -1, head_size)
    half = head_size // 2
    freq = 10000.0 ** (-jnp.arange(half, dtype=jnp.float32) / half)
    angle = position[:, None, None] * freq[None, None, :]
    cosine = jnp.cos(angle)
    sine = jnp.sin(angle)
    first = shaped[..., :half]
    second = shaped[..., half:]
    turned = jnp.concatenate(
        [first * cosine - second * sine, second * cosine + first * sine], axis=-1
    )
    return turned.reshape(count, -1)


def layout(lengths, cached, split_flag, prev_len, count):
    ends = jnp.cumsum(lengths)
    starts = ends - lengths
    place = jnp.arange(count, dtype=jnp.int32)
    member = ((place[:, None] >= starts[None, :]) & (place[:, None] < ends[None, :])).astype(
        jnp.int32
    )
    request = jnp.sum(member * jnp.arange(lengths.shape[0], dtype=jnp.int32)[None, :], axis=1)
    offset = place - jnp.sum(member * starts[None, :], axis=1)
    extra = jnp.where(request == 0, split_flag * prev_len, 0)
    position = jnp.sum(member * cached[None, :], axis=1) + extra + offset
    return (member, request, position.astype(jnp.float32))


def attend(
    query_vectors,
    keys,
    values,
    prev_keys,
    prev_values,
    cache_keys,
    cache_values,
    request,
    cached,
    split_flag,
    prev_len,
    head_size,
):
    count = query_vectors.shape[0]
    kv_heads = keys.shape[1] // head_size
    ratio = query_vectors.shape[1] // keys.shape[1]
    block = cache_keys.shape[1]
    slots = cache_keys.shape[0] * block
    every_key = jnp.concatenate([cache_keys.reshape(slots, -1), prev_keys, keys], 0).reshape(
        -1, kv_heads, head_size
    )
    every_value = jnp.concatenate(
        [cache_values.reshape(slots, -1), prev_values, values], 0
    ).reshape(-1, kv_heads, head_size)
    slot_req = jnp.arange(slots, dtype=jnp.int32) // block
    slot_col = jnp.arange(slots, dtype=jnp.int32) % block
    cache_ok = (request[:, None] == slot_req[None, :]) & (
        slot_col[None, :] < cached[slot_req][None, :]
    )
    place = jnp.arange(count, dtype=jnp.int32)
    prev_ok = (split_flag == 1) & (request[:, None] == 0) & (place[None, :] >= count - prev_len)
    own_ok = (request[:, None] == request[None, :]) & (place[None, :] <= place[:, None])
    allowed = jnp.concatenate([cache_ok, prev_ok, own_ok], 1)
    grouped = query_vectors.reshape(count, kv_heads, ratio, head_size)
    scores = jnp.einsum(
        "tkrd,skd->krts", grouped, every_key, preferred_element_type=jnp.float32
    ) * head_size ** (-0.5)
    scores = jnp.where(allowed[None, None], scores, jnp.float32(-1e30))
    top = jnp.max(scores, axis=-1, keepdims=True)
    weights = jnp.exp(scores - top)
    total = jnp.sum(weights, axis=-1)
    numer = jnp.einsum(
        "krts,skd->tkrd",
        weights.astype(jnp.bfloat16),
        every_value,
        preferred_element_type=jnp.float32,
    )
    result = numer / jnp.transpose(total, (2, 0, 1))[..., None]
    return result.reshape(count, -1).astype(jnp.bfloat16)


def on_device(
    stream,
    prenorm_gain,
    query_weight,
    key_weight,
    value_weight,
    output_weight,
    adapter_down_rows,
    adapter_up_query,
    request_adapter,
    adapter_row_index,
    request_token_length,
    continues_previous,
    request_cache_block,
    cached_length,
    cached_rotated_keys,
    cached_value_rows,
):
    count = stream.shape[0]
    width = stream.shape[1]
    group_at = lax.axis_index("group")
    model_at = lax.axis_index("mp")
    whole = lax.all_gather(stream, "mp", axis=1, tiled=True)
    wide = whole.astype(jnp.float32)
    normalized_input = (
        wide * lax.rsqrt(jnp.mean(wide * wide, axis=1, keepdims=True) + 1e-06) * prenorm_gain
    ).astype(jnp.bfloat16)
    normed_part = lax.dynamic_slice_in_dim(normalized_input, model_at * width, width, 1)
    before = jnp.maximum(group_at - 1, 0)
    lengths = request_token_length[group_at]
    cached = cached_length[group_at]
    split_flag = continues_previous[group_at]
    prev_len = request_token_length[before, REQS - 1]
    member, request, position = layout(lengths, cached, split_flag, prev_len, count)
    wanted = adapter_row_index[request_adapter[group_at]]
    pieces = (
        lax.all_gather(adapter_down_rows, "group", axis=0, tiled=True),
        lax.all_gather(adapter_up_query, "group", axis=0, tiled=True),
    )
    stored = jnp.arange(pieces[0].shape[0], dtype=jnp.int32)
    onehot = (wanted[:, None] == stored[None, :]).astype(jnp.bfloat16)
    new_down = jnp.einsum("rj,jkd->rkd", onehot, pieces[0], preferred_element_type=jnp.float32)
    new_up = jnp.einsum("rj,jkd->rkd", onehot, pieces[1], preferred_element_type=jnp.float32)
    chosen_down = new_down.astype(jnp.bfloat16)
    chosen_up = new_up.astype(jnp.bfloat16)
    rank_index = adapter_down_rows.shape[1]
    partial_low = jnp.einsum(
        "td,rkd->trk", normed_part, chosen_down, preferred_element_type=jnp.float32
    ).reshape(count, REQS * rank_index)
    low = lax.psum(partial_low, "mp").astype(jnp.bfloat16)
    own_columns = jnp.repeat(member, rank_index, axis=1).astype(jnp.bfloat16)
    query_update = jnp.dot(
        low * own_columns,
        chosen_up.reshape(REQS * rank_index, -1),
        preferred_element_type=jnp.float32,
    )
    query_vectors = (
        jnp.dot(normalized_input, query_weight, preferred_element_type=jnp.float32)
        + adapter_scale * query_update
    )
    query_vectors = rotate(query_vectors, position, HEAD_WIDTH).astype(jnp.bfloat16)
    keys = rotate(
        jnp.dot(normalized_input, key_weight, preferred_element_type=jnp.float32),
        position,
        HEAD_WIDTH,
    ).astype(jnp.bfloat16)
    values = jnp.dot(normalized_input, value_weight, preferred_element_type=jnp.float32).astype(
        jnp.bfloat16
    )
    prev_keys, prev_values = shifted((keys, values), "group", 1)
    blocks = request_cache_block[group_at]
    pieces = (
        lax.all_gather(cached_rotated_keys, "group", axis=0, tiled=True),
        lax.all_gather(cached_value_rows, "group", axis=0, tiled=True),
    )
    stored = jnp.arange(pieces[0].shape[0], dtype=jnp.int32)
    onehot = (blocks[:, None] == stored[None, :]).astype(jnp.bfloat16)
    new_keys = jnp.einsum("rj,jcd->rcd", onehot, pieces[0], preferred_element_type=jnp.float32)
    new_values = jnp.einsum("rj,jcd->rcd", onehot, pieces[1], preferred_element_type=jnp.float32)
    cache_keys = new_keys.astype(jnp.bfloat16)
    cache_values = new_values.astype(jnp.bfloat16)
    attended = attend(
        query_vectors,
        keys,
        values,
        prev_keys,
        prev_values,
        cache_keys,
        cache_values,
        request,
        cached,
        split_flag,
        prev_len,
        HEAD_WIDTH,
    )
    partial_out = jnp.dot(attended, output_weight, preferred_element_type=jnp.float32)
    return lax.psum_scatter(partial_out.astype(jnp.bfloat16), "mp", scatter_dimension=1, tiled=True)


def solution(mesh):
    placed = (
        P("group", "mp"),
        P(),
        P(None, "mp"),
        P(None, "mp"),
        P(None, "mp"),
        P("mp", None),
        P("group", None, "mp"),
        P("group", None, "mp"),
        P(),
        P(),
        P(),
        P(),
        P(),
        P(),
        P("group", None, "mp"),
        P("group", None, "mp"),
    )
    return jax.shard_map(
        on_device, mesh=mesh, in_specs=placed, out_specs=P("group", "mp"), check_vma=False
    )
```

profile of v0, /device:TPU:0, one launch (start us, length us, event | category | flops | bytes accessed | tf_op | source)
XLA Modules:
  0.0 254.0 jit_solution(16617972660007501374)
XLA Ops:
  13.4 26.9 %all_gather.18 = bf16[64,16,448]{2,1,0:T(8,128)(2,1)S(1)} all-gather(bf16[4,16,448]{2,1,0:T(8,128)(2,1)} %param.22), channel_id=1, replica_groups=mesh['group'=16,'mp'=8] {'group'}, dimensions={0}, use_global_device_ids=true | all-gather | bytes 974848 | tf_op jit(solution)/shard_map/all_gather | solution.py:135
  40.9 2.6 %compare_select_fusion.1 = s32[1024,1]{0,1:T(1,128)S(1)} fusion(s32[]{:T(128)} %bitcast.7, s32[]{:T(128)} %bitcast.8, s32[]{:T(128)} %bitcast.10, s32[]{:T(128)} %bitcast.9), kind=kLoop, calls=%fused_computation.71 | loop fusion | flops 17408 | bytes 4112 | tf_op jit(solution)/shard_map/gather | solution.py:75
  49.5 1.8 multiply_cosine_fusion
  54.9 2.4 convolution_convert_fusion.2
  57.4 28.5 %all-gather.7.cloned.1.call-done = bf16[512,3584]{0,1:T(8,128)(2,1)} async-done(((bf16[512,448]{0,1:T(8,128)(2,1)}), bf16[512,3584]{0,1:T(8,128)(2,1)}) %all-gather.7.cloned.1.call-update) | async-done | bytes 3670032 | tf_op jit(solution)/shard_map/all_gather | solution.py:121
  85.8 3.0 %fusion.2 = f32[512]{0:T(512)S(1)} fusion(bf16[512,3584]{0,1:T(8,128)(2,1)} %all-gather.7.cloned.1.call-done), kind=kLoop, calls=%fused_computation.7 | loop fusion | flops 5504512 | bytes 3672064 | tf_op jit(solution)/shard_map/reduce_sum | solution.py:124
  90.6 1.8 copy-done.2
  92.4 1.9 convolution_convert_fusion.1
  96.1 4.2 %collective-permute-start = (bf16[512,256]{1,0:T(8,128)(2,1)}, bf16[512,256]{1,0:T(8,128)(2,1)}, u32[]{:S(2)}, u32[]{:S(2)}) collective-permute-start(bf16[512,256]{1,0:T(8,128)(2,1)} %convolution_convert_fusion.1), channel_id=1, source_target_pairs={{0,8},{8,16},{16,24},{24,32},{32,40},{40,48},{48,56},{56,64},{64,7... | collective-permute-start | bytes 786440 | tf_op jit(solution)/shard_map/ppermute | solution.py:14
  100.2 3.8 %convolution_bitcast_fusion = f32[512,1,256]{0,2,1:T(8,128)S(1)} fusion(bf16[512,3584]{0,1:T(8,128)(2,1)} %copy-done.2, bf16[3584,256]{1,0:T(8,128)(2,1)} %param.19), kind=kOutput, calls=%fused_computation.26 | convolution fusion | flops 939524096 | bytes 6029312 | tf_op jit(solution)/shard_map/dot_general | solution.py:161
  107.7 3.4 %collective-permute-start.1 = (bf16[512,256]{0,1:T(8,128)(2,1)}, bf16[512,256]{0,1:T(8,128)(2,1)}, u32[]{:S(2)}, u32[]{:S(2)}) collective-permute-start(bf16[512,256]{0,1:T(8,128)(2,1)} %maximum_bitcast_fusion.6), channel_id=1, source_target_pairs={{0,8},{8,16},{16,24},{24,32},{32,40},{40,48},{48,56},{56,64},{64,7... | collective-permute-start | bytes 786440 | tf_op jit(solution)/shard_map/ppermute | solution.py:14
  112.3 26.0 %all-reduce.1 = bf16[512,64]{0,1:T(8,128)(2,1)S(1)} all-reduce(f32[512,64]{0,1:T(8,128)S(1)} %bitcast.101), channel_id=1, replica_groups=mesh['group'=16,'mp'=8] {'mp'}, use_global_device_ids=true, to_apply=%region_5.6 | all-reduce | flops 32768 | bytes 196608 | tf_op jit(solution)/shard_map/psum | solution.py:148
  138.4 5.3 %fusion.82 = f32[512,512]{0,1:T(8,128)S(1)} fusion(bf16[512,3584]{0,1:T(8,128)(2,1)} %copy-done.2, bf16[3584,512]{1,0:T(8,128)(2,1)} %param.18), kind=kOutput, calls=%fused_computation.129 | convolution fusion | flops 1879048192 | bytes 8388608 | tf_op jit(solution)/shard_map/dot_general | solution.py:156
  146.4 2.1 copy.62
  148.5 2.2 subtract_convert_fusion
  150.6 1.8 copy.46
  154.3 4.6 %fusion.18 = bf16[4,256,256]{2,0,1:T(4,128)(2,1)S(1)} fusion(bf16[32,256,256]{2,1,0:T(8,128)(2,1)} %all-gather.5.cloned.1.call-done, s32[4]{0:T(128)S(1)} %dynamic-slice_reduce_fusion.1), kind=kOutput, calls=%fused_computation.24 | convolution fusion | flops 17039488 | bytes 4718608 | tf_op jit(solution)/shard_map/rj,jcd->rcd/dot_general | solution.py:177
  160.0 35.3 %all-gather.9.cloned.1.call-done = bf16[32,256,256]{2,1,0:T(8,128)(2,1)} async-done(((bf16[2,256,256]{2,1,0:T(8,128)(2,1)}), bf16[32,256,256]{2,1,0:T(8,128)(2,1)}) %all-gather.9.cloned.1.call-update) | async-done | bytes 4194320 | tf_op jit(solution)/shard_map/all_gather | solution.py:171
  195.3 4.7 %fusion.21 = bf16[4,256,256]{2,0,1:T(4,128)(2,1)S(1)} fusion(bf16[32,256,256]{2,1,0:T(8,128)(2,1)} %all-gather.9.cloned.1.call-done, s32[4]{0:T(128)S(1)} %dynamic-slice_reduce_fusion.1), kind=kOutput, calls=%fused_computation.25 | convolution fusion | flops 17039488 | bytes 4718608 | tf_op jit(solution)/shard_map/rj,jcd->rcd/dot_general | solution.py:176
  200.1 1.8 fusion.5
  201.9 2.2 fusion
  204.2 2.8 %divide_convert_fusion = bf16[512,1,2,256]{0,3,2,1:T(8,128)(2,1)S(1)} fusion(f32[2048,512,2]{1,0,2:T(8,128)S(1)} %get-tuple-element.25, f32[2,512]{1,0:T(2,128)S(1)} %get-tuple-element.24, pred[512,2048]{0,1:T(8,128)(4,1)S(1)} %pad_add_fusion, bf16[512,256]{0,1:T(8,128)(2,1)S(1)} %copy-done.4, bf16[512,256]{0,1:T(8,128)(2,1)S(1)} %copy-done.6, ...), kind=kOutput, calls=%fused_computation.43 | convolution fusion | flops 1085800448 | bytes 11018240 | tf_op jit(solution)/shard_map/krts,skd->tkrd/dot_general | solution.py:89
  207.0 3.9 %convolution_convert_fusion = bf16[512,3584]{0,1:T(8,128)(2,1)} fusion(bf16[512,512]{0,1:T(8,128)(2,1)S(1)} %bitcast.107, bf16[512,3584]{1,0:T(8,128)(2,1)S(1)} %copy-done.11), kind=kOutput, calls=%fused_computation.11 | convolution fusion | flops 1880883200 | bytes 7864320 | tf_op jit(solution)/shard_map/dot_general | solution.py:194
  210.9 36.5 %reduce-scatter.2.cloned.1.call-done = bf16[512,448]{0,1:T(8,128)(2,1)} async-done(((bf16[512,3584]{0,1:T(8,128)(2,1)}), bf16[512,448]{0,1:T(8,128)(2,1)}) %reduce-scatter.2.cloned.1.call-update) | async-done | bytes 458768 | tf_op jit(solution)/shard_map/reduce_scatter | solution.py:195
  (78 shorter events, 28.4 us)
Async XLA Ops:
  6.5 85.8 %copy-start = (bf16[3584,256]{1,0:T(8,128)(2,1)S(1)}, bf16[3584,256]{1,0:T(8,128)(2,1)}, u32[]{:S(2)}) copy-start(bf16[3584,256]{1,0:T(8,128)(2,1)} %param.20) | copy-start | bytes 5505028
  6.5 48.4 %all-gather.11.cloned.1.call-start = ((), (), s32[]{:S(2)}) async-start(), calls=%async_computation.4 | async-start | bytes 1114112 | tf_op jit(solution)/shard_map/all_gather | solution.py:136
  7.3 78.6 %all-gather.7.cloned.1.call-start = ((), (), s32[]{:S(2)}) async-start(), calls=%async_computation.2 | async-start | bytes 4128768 | tf_op jit(solution)/shard_map/all_gather | solution.py:121
  8.0 146.3 %all-gather.5.cloned.1.call-start = ((), (), s32[]{:S(2)}) async-start(), calls=%async_computation.1 | async-start | bytes 4456448 | tf_op jit(solution)/shard_map/all_gather | solution.py:172
  8.7 186.5 %all-gather.9.cloned.1.call-start = ((), (), s32[]{:S(2)}) async-start(), calls=%async_computation.3 | async-start | bytes 4456448 | tf_op jit(solution)/shard_map/all_gather | solution.py:171
  9.3 238.1 %reduce-scatter.2.cloned.1.call-start = ((), (), s32[]{:S(2)}) async-start(), calls=%async_computation.5 | async-start | bytes 4128768 | tf_op jit(solution)/shard_map/reduce_scatter | solution.py:195
  53.4 35.5 %copy-start.10 = (f32[3584]{0:T(1024)S(1)}, f32[3584]{0:T(1024)}, u32[]{:S(2)}) copy-start(f32[3584]{0:T(1024)} %param.17) | copy-start | bytes 43012
  85.8 3.1 %copy-start.1 = (bf16[512,3584]{0,1:T(8,128)(2,1)S(1)}, bf16[512,3584]{0,1:T(8,128)(2,1)}, u32[]{:S(2)}) copy-start(bf16[512,3584]{0,1:T(8,128)(2,1)} %all-gather.7.cloned.1.call-done) | copy-start | bytes 11010052
  90.5 1.8 copy-start.2
  96.1 54.6 %collective-permute-start = (bf16[512,256]{1,0:T(8,128)(2,1)}, bf16[512,256]{1,0:T(8,128)(2,1)}, u32[]{:S(2)}, u32[]{:S(2)}) collective-permute-start(bf16[512,256]{1,0:T(8,128)(2,1)} %convolution_convert_fusion.1), channel_id=1, source_target_pairs={{0,8},{8,16},{16,24},{24,32},{32,40},{40,48},{48,56},{56,64},{64,7... | collective-permute-start | bytes 786440 | tf_op jit(solution)/shard_map/ppermute | solution.py:14
  107.7 44.8 %collective-permute-start.1 = (bf16[512,256]{0,1:T(8,128)(2,1)}, bf16[512,256]{0,1:T(8,128)(2,1)}, u32[]{:S(2)}, u32[]{:S(2)}) collective-permute-start(bf16[512,256]{0,1:T(8,128)(2,1)} %maximum_bitcast_fusion.6), channel_id=1, source_target_pairs={{0,8},{8,16},{16,24},{24,32},{32,40},{40,48},{48,56},{56,64},{64,7... | collective-permute-start | bytes 786440 | tf_op jit(solution)/shard_map/ppermute | solution.py:14
  160.0 40.1 %copy-start.5 = (bf16[512,256]{1,0:T(8,128)(2,1)S(1)}, bf16[512,256]{1,0:T(8,128)(2,1)}, u32[]{:S(2)}) copy-start(bf16[512,256]{1,0:T(8,128)(2,1)} %copy.52) | copy-start | bytes 786436
  160.0 40.1 %copy-start.7 = (bf16[512,256]{1,0:T(8,128)(2,1)S(1)}, bf16[512,256]{1,0:T(8,128)(2,1)}, u32[]{:S(2)}) copy-start(bf16[512,256]{1,0:T(8,128)(2,1)} %copy.51) | copy-start | bytes 786436
  195.3 4.8 %copy-start.8 = (bf16[512,2,128]{2,0,1:T(8,128)(2,1)S(1)}, bf16[512,2,128]{2,0,1:T(8,128)(2,1)}, u32[]{:S(2)}) copy-start(bf16[512,2,128]{2,0,1:T(8,128)(2,1)} %get-tuple-element.12) | copy-start | bytes 786436
  195.3 4.8 %copy-start.9 = (bf16[512,2,128]{2,0,1:T(8,128)(2,1)S(1)}, bf16[512,2,128]{2,0,1:T(8,128)(2,1)}, u32[]{:S(2)}) copy-start(bf16[512,2,128]{2,0,1:T(8,128)(2,1)} %get-tuple-element.13) | copy-start | bytes 786436
  201.9 2.2 copy-start.3
  201.9 2.2 copy-start.4
  201.9 2.2 copy-start.6
  204.2 2.8 %copy-start.11 = (bf16[512,3584]{1,0:T(8,128)(2,1)S(1)}, bf16[512,3584]{1,0:T(8,128)(2,1)}, u32[]{:S(2)}) copy-start(bf16[512,3584]{1,0:T(8,128)(2,1)} %param.21) | copy-start | bytes 11010052
Sparse Core Ops, SparseCore 0:
  9.5 45.3 all-gather.10
  56.6 29.1 all-gather.6
  88.0 53.9 all-gather.4
  144.0 51.2 all-gather.8
  211.0 36.3 reduce-scatter.1
where the time goes:
time: 255 us; the launch traced here: 254 us
  waiting for transfers between devices  104 us (41%)
  blocking collectives  52.9 us (21%)
  matrix products  33.9 us (13%)
  local copies, waits for them, and re-layouts  21.9 us (9%)
  other arithmetic  17.3 us (7%)
  between operations  16.1 us (6%)
  starting transfers between devices  7.77 us (3%)
    reduce_scatter x1, waiting for transfers between devices, on_device(): lax.psum_scatter(partial_out.astype(jnp.bfloat16), 'mp', scatter_dimensio...  36.5 us
    all_gather x1, waiting for transfers between devices, on_device(): lax.all_gather(cached_rotated_keys, 'group', axis=0, tiled=True)  35.3 us
    all_gather x1, waiting for transfers between devices, on_device(): whole = lax.all_gather(stream, 'mp', axis=1, tiled=True)  28.5 us
    all_gather x1, blocking collectives, on_device(): lax.all_gather(adapter_down_rows, 'group', axis=0, tiled=True)  26.9 us
    psum x1, blocking collectives, on_device(): low = lax.psum(partial_low, 'mp').astype(jnp.bfloat16)  26 us
    ppermute x2, starting transfers between devices, shifted(): lax.ppermute(value, axis, [(source, source + steps) for source in range(f...  7.62 us
    unnamed x27, local copies, waits for them, and re-layouts  5.37 us
    dot_general x1, matrix products, on_device(): jnp.dot(normalized_input, query_weight, preferred_element_type=jnp.float32)  5.26 us
  transfers between devices with their start and end apart: 7, of which 4 were waited for; matrix products, arithmetic and copies ran while one was open for 22% of the time, Pallas kernels for 0%

commit v1 on v0

--- a/solution.py
+++ b/solution.py
@@ -118,7 +118,12 @@
     width = stream.shape[1]
     group_at = lax.axis_index("group")
     model_at = lax.axis_index("mp")
-    whole = lax.all_gather(stream, "mp", axis=1, tiled=True)
+    ring = [stream]
+    for hop in range(7):
+        ring.append(lax.ppermute(ring[-1], "mp", [(dev, (dev + 1) % 8) for dev in range(8)]))
+    whole = jnp.roll(
+        jnp.concatenate(ring[::-1], axis=1), (lax.axis_index("mp") + 1) * ring[0].shape[1], axis=1
+    )
     wide = whole.astype(jnp.float32)
     normalized_input = (
         wide * lax.rsqrt(jnp.mean(wide * wide, axis=1, keepdims=True) + 1e-06) * prenorm_gain

time: 255 us -> 243 us (0.953)
  waiting for transfers between devices: 104 us -> 77.8 us
  local copies, waits for them, and re-layouts: 21.9 us -> 36.1 us
    ppermute x0 -> x7, waiting for transfers between devices: none -> 40.8 us  [on_device(): lax.ppermute(ring[-1], 'mp', [(dev, (dev + 1) % 8) for dev in range(8)])]
    all_gather x1, waiting for transfers between devices: 35.3 us -> 0.01 us  [on_device(): lax.all_gather(cached_rotated_keys, 'group', axis=0, tiled=True)]
    all_gather x1 -> x0, waiting for transfers between devices: 28.5 us -> none  [on_device(): whole = lax.all_gather(stream, 'mp', axis=1, tiled=True)]
    unnamed x27 -> x42, local copies, waits for them, and re-layouts: 5.37 us -> 18.8 us
    dot_general x1, matrix products: 3.76 us -> 1.16 us  [on_device(): jnp.dot(normalized_input, key_weight, preferred_element_type=jnp.float32)]
    dot_general x1, matrix products: 1.89 us -> 4.48 us  [on_device(): jnp.dot(normalized_input, value_weight, preferred_element_type=jnp.float32)]
  transfers between devices with their start and end apart: 7 -> 13, of which waited for: 4 -> 7; matrix products, arithmetic and copies ran while one was open for 22% -> 28% of each run, Pallas kernels for 0% -> 0%
where the time goes in v1:
time: 243 us; the launch traced here: 242 us
  waiting for transfers between devices  77.8 us (32%)
  blocking collectives  52.7 us (22%)
  local copies, waits for them, and re-layouts  36.1 us (15%)
  matrix products  35.6 us (15%)
  other arithmetic  17.3 us (7%)
  between operations  16.2 us (7%)
  starting transfers between devices  6.16 us (3%)
    ppermute x7, waiting for transfers between devices, on_device(): lax.ppermute(ring[-1], 'mp', [(dev, (dev + 1) % 8) for dev in range(8)])  40.8 us
    reduce_scatter x1, waiting for transfers between devices, on_device(): lax.psum_scatter(partial_out.astype(jnp.bfloat16), 'mp', scatter_dimensio...  35 us
    all_gather x1, blocking collectives, on_device(): lax.all_gather(adapter_down_rows, 'group', axis=0, tiled=True)  27 us
    psum x1, blocking collectives, on_device(): low = lax.psum(partial_low, 'mp').astype(jnp.bfloat16)  25.7 us
    unnamed x42, local copies, waits for them, and re-layouts  18.8 us
    ppermute x2, starting transfers between devices, shifted(): lax.ppermute(value, axis, [(source, source + steps) for source in range(f...  5.99 us
    dot_general x1, matrix products, on_device(): jnp.dot(normalized_input, query_weight, preferred_element_type=jnp.float32)  5.26 us
  transfers between devices with their start and end apart: 13, of which 7 were waited for; matrix products, arithmetic and copies ran while one was open for 28% of the time, Pallas kernels for 0%

profile of v1, /device:TPU:0, one launch (start us, length us, event | category | flops | bytes accessed | tf_op | source)
XLA Modules:
  0.0 241.9 jit_solution(14970009428331778092)
XLA Ops:
  11.5 2.6 %compare_select_fusion.1 = s32[1024,1]{0,1:T(1,128)S(1)} fusion(s32[]{:T(128)} %bitcast.7, s32[]{:T(128)} %bitcast.8, s32[]{:T(128)} %bitcast.10, s32[]{:T(128)} %bitcast.9), kind=kLoop, calls=%fused_computation.87 | loop fusion | flops 17408 | bytes 4112 | tf_op jit(solution)/shard_map/gather | solution.py:75
  16.1 27.0 %all_gather.14 = bf16[64,16,448]{2,1,0:T(8,128)(2,1)S(1)} all-gather(bf16[4,16,448]{2,1,0:T(8,128)(2,1)} %param.22), channel_id=1, replica_groups=mesh['group'=16,'mp'=8] {'group'}, dimensions={0}, use_global_device_ids=true | all-gather | bytes 974848 | tf_op jit(solution)/shard_map/all_gather | solution.py:140
  48.3 4.0 %collective-permute-done.1 = bf16[512,448]{0,1:T(8,128)(2,1)} collective-permute-done((bf16[512,448]{0,1:T(8,128)(2,1)S(1)}, bf16[512,448]{0,1:T(8,128)(2,1)}, u32[]{:S(2)}, u32[]{:S(2)}) %collective-permute-start.1) | collective-permute-done | bytes 458784 | tf_op jit(solution)/shard_map/ppermute | solution.py:123
  54.2 7.5 %collective-permute-done.2 = bf16[512,448]{0,1:T(8,128)(2,1)S(1)} collective-permute-done((bf16[512,448]{0,1:T(8,128)(2,1)}, bf16[512,448]{0,1:T(8,128)(2,1)S(1)}, u32[]{:S(2)}, u32[]{:S(2)}) %collective-permute-start.2) | collective-permute-done | bytes 458784 | tf_op jit(solution)/shard_map/ppermute | solution.py:123
  63.2 7.6 %collective-permute-done.3 = bf16[512,448]{0,1:T(8,128)(2,1)} collective-permute-done((bf16[512,448]{0,1:T(8,128)(2,1)S(1)}, bf16[512,448]{0,1:T(8,128)(2,1)}, u32[]{:S(2)}, u32[]{:S(2)}) %collective-permute-start.3) | collective-permute-done | bytes 458784 | tf_op jit(solution)/shard_map/ppermute | solution.py:123
  73.4 6.9 %collective-permute-done.4 = bf16[512,448]{0,1:T(8,128)(2,1)} collective-permute-done((bf16[512,448]{0,1:T(8,128)(2,1)}, bf16[512,448]{0,1:T(8,128)(2,1)}, u32[]{:S(2)}, u32[]{:S(2)}) %collective-permute-start.4) | collective-permute-done | bytes 458784 | tf_op jit(solution)/shard_map/ppermute | solution.py:123
  81.8 7.9 %collective-permute-done.5 = bf16[512,448]{0,1:T(8,128)(2,1)} collective-permute-done((bf16[512,448]{0,1:T(8,128)(2,1)}, bf16[512,448]{0,1:T(8,128)(2,1)}, u32[]{:S(2)}, u32[]{:S(2)}) %collective-permute-start.5) | collective-permute-done | bytes 458784 | tf_op jit(solution)/shard_map/ppermute | solution.py:123
  89.8 2.5 %convolution_convert_fusion.2 = bf16[4,16,512]{2,0,1:T(4,128)(2,1)S(1)} fusion(bf16[64,16,512]{2,1,0:T(8,128)(2,1)} %all-gather.8.cloned.1.call-done, s32[4]{0:T(128)S(1)} %gather_fusion), kind=kOutput, calls=%fused_computation.28 | convolution fusion | flops 4227328 | bytes 1114128 | tf_op jit(solution)/shard_map/rj,jkd->rkd/dot_general | solution.py:146
  92.3 6.8 %collective-permute-done.6 = bf16[512,448]{0,1:T(8,128)(2,1)} collective-permute-done((bf16[512,448]{0,1:T(8,128)(2,1)}, bf16[512,448]{0,1:T(8,128)(2,1)}, u32[]{:S(2)}, u32[]{:S(2)}) %collective-permute-start.6) | collective-permute-done | bytes 458784 | tf_op jit(solution)/shard_map/ppermute | solution.py:123
  115.1 1.9 copy-done.1
  120.1 3.9 %collective-permute-start.8 = (bf16[512,256]{0,1:T(8,128)(2,1)}, bf16[512,256]{0,1:T(8,128)(2,1)}, u32[]{:S(2)}, u32[]{:S(2)}) collective-permute-start(bf16[512,256]{0,1:T(8,128)(2,1)} %maximum_bitcast_fusion.6), channel_id=1, source_target_pairs={{0,8},{8,16},{16,24},{24,32},{32,40},{40,48},{48,56},{56,64},{64,7... | collective-permute-start | bytes 786440 | tf_op jit(solution)/shard_map/ppermute | solution.py:14
  125.8 4.5 %convolution_convert_fusion.1 = bf16[512,256]{1,0:T(8,128)(2,1)} fusion(bf16[512,3584]{0,1:T(8,128)(2,1)} %copy-done.1, bf16[3584,256]{1,0:T(8,128)(2,1)} %param.20), kind=kOutput, calls=%fused_computation.27 | convolution fusion | flops 939655168 | bytes 5767168 | tf_op jit(solution)/shard_map/dot_general | solution.py:170
  130.3 2.1 collective-permute-start.7
  135.4 25.7 %all-reduce.1 = bf16[512,64]{0,1:T(8,128)(2,1)S(1)} all-reduce(f32[512,64]{0,1:T(8,128)S(1)} %bitcast.101), channel_id=1, replica_groups=mesh['group'=16,'mp'=8] {'mp'}, use_global_device_ids=true, to_apply=%region_5.6 | all-reduce | flops 32768 | bytes 196608 | tf_op jit(solution)/shard_map/psum | solution.py:153
  161.4 5.3 %convolution_add_fusion = f32[512,512]{0,1:T(8,128)S(1)} fusion(f32[512,512]{0,1:T(8,128)S(1)} %convolution_multiply_fusion, bf16[512,3584]{0,1:T(8,128)(2,1)} %copy-done.1, bf16[3584,512]{1,0:T(8,128)(2,1)} %param.18), kind=kOutput, calls=%fused_computation.23 | convolution fusion | flops 1879310336 | bytes 9437184 | tf_op jit(solution)/shard_map/dot_general | solution.py:161
  169.0 2.0 copy.63
  171.1 2.1 subtract_convert_fusion
  176.7 4.6 %fusion.20 = bf16[4,256,256]{2,0,1:T(4,128)(2,1)S(1)} fusion(bf16[32,256,256]{2,1,0:T(8,128)(2,1)} %all-gather.6.cloned.1.call-done, s32[4]{0:T(128)S(1)} %dynamic-slice_reduce_fusion.1), kind=kOutput, calls=%fused_computation.25 | convolution fusion | flops 17039488 | bytes 4718608 | tf_op jit(solution)/shard_map/rj,jcd->rcd/dot_general | solution.py:181
  182.2 4.6 %fusion.17 = bf16[4,256,256]{2,0,1:T(4,128)(2,1)S(1)} fusion(bf16[32,256,256]{2,1,0:T(8,128)(2,1)} %all-gather.4.cloned.1.call-done, s32[4]{0:T(128)S(1)} %dynamic-slice_reduce_fusion.1), kind=kOutput, calls=%fused_computation.24 | convolution fusion | flops 17039488 | bytes 4718608 | tf_op jit(solution)/shard_map/rj,jcd->rcd/dot_general | solution.py:182
  188.0 3.5 %fusion.5 = (f32[2,512]{1,0:T(2,128)S(1)}, f32[2048,512,2]{1,0,2:T(8,128)S(1)}) fusion(pred[512,2048]{0,1:T(8,128)(4,1)S(1)} %pad_add_fusion, bf16[512,2,128]{2,0,1:T(8,128)(2,1)} %get-tuple-element.13, bf16[512,2,128]{2,0,1:T(8,128)(2,1)} %get-tuple-element.12, bf16[512,256]{1,0:T(8,128)(2,1)} %copy.52, bf16[512,256]{1,0:T(8,128)(2,1)} %copy.51, ...), kind=kOutput, calls=%fused_computation.10 | convolution fusion | flops 1084226560 | bytes 11014144 | tf_op jit(solution)/shard_map/tkrd,skd->krts/dot_general | solution.py:82
  191.4 2.2 fusion
  193.7 2.8 %divide_convert_fusion = bf16[512,1,2,256]{0,3,2,1:T(8,128)(2,1)S(1)} fusion(f32[2048,512,2]{1,0,2:T(8,128)S(1)} %get-tuple-element.25, f32[2,512]{1,0:T(2,128)S(1)} %get-tuple-element.24, pred[512,2048]{0,1:T(8,128)(4,1)S(1)} %pad_add_fusion, bf16[512,256]{0,1:T(8,128)(2,1)S(1)} %copy-done.8, bf16[512,256]{0,1:T(8,128)(2,1)S(1)} %copy-done.9, ...), kind=kOutput, calls=%fused_computation.43 | convolution fusion | flops 1085800448 | bytes 11018240 | tf_op jit(solution)/shard_map/krts,skd->tkrd/dot_general | solution.py:89
  196.5 3.9 %convolution_convert_fusion = bf16[512,3584]{0,1:T(8,128)(2,1)} fusion(bf16[512,512]{0,1:T(8,128)(2,1)S(1)} %bitcast.107, bf16[512,3584]{1,0:T(8,128)(2,1)S(1)} %copy-done.11), kind=kOutput, calls=%fused_computation.11 | convolution fusion | flops 1880883200 | bytes 7864320 | tf_op jit(solution)/shard_map/dot_general | solution.py:199
  200.4 35.0 %reduce-scatter.2.cloned.1.call-done = bf16[512,448]{0,1:T(8,128)(2,1)} async-done(((bf16[512,3584]{0,1:T(8,128)(2,1)}), bf16[512,448]{0,1:T(8,128)(2,1)}) %reduce-scatter.2.cloned.1.call-update) | async-done | bytes 458768 | tf_op jit(solution)/shard_map/reduce_scatter | solution.py:200
  (105 shorter events, 48.8 us)
Async XLA Ops:
  6.5 110.5 %copy-start = (bf16[3584,256]{1,0:T(8,128)(2,1)S(1)}, bf16[3584,256]{1,0:T(8,128)(2,1)}, u32[]{:S(2)}) copy-start(bf16[3584,256]{1,0:T(8,128)(2,1)} %param.19) | copy-start | bytes 5505028
  6.5 83.3 %all-gather.8.cloned.1.call-start = ((), (), s32[]{:S(2)}) async-start(), calls=%async_computation.3 | async-start | bytes 1114112 | tf_op jit(solution)/shard_map/all_gather | solution.py:141
  7.3 169.5 %all-gather.6.cloned.1.call-start = ((), (), s32[]{:S(2)}) async-start(), calls=%async_computation.2 | async-start | bytes 4456448 | tf_op jit(solution)/shard_map/all_gather | solution.py:176
  8.0 174.2 %all-gather.4.cloned.1.call-start = ((), (), s32[]{:S(2)}) async-start(), calls=%async_computation.1 | async-start | bytes 4456448 | tf_op jit(solution)/shard_map/all_gather | solution.py:177
  8.1 35.0 %collective-permute-start = (bf16[512,448]{0,1:T(8,128)(2,1)}, bf16[512,448]{0,1:T(8,128)(2,1)S(1)}, u32[]{:S(2)}, u32[]{:S(2)}) collective-permute-start(bf16[512,448]{0,1:T(8,128)(2,1)} %param.16), channel_id=1, source_target_pairs={{0,1},{1,2},{2,3},{3,4},{4,5},{5,6},{6,7},{7,0},{8,9},{9,10},{10,1... | collective-permute-start | bytes 1376264 | tf_op jit(solution)/shard_map/ppermute | solution.py:123
  8.7 226.7 %reduce-scatter.2.cloned.1.call-start = ((), (), s32[]{:S(2)}) async-start(), calls=%async_computation.4 | async-start | bytes 4128768 | tf_op jit(solution)/shard_map/reduce_scatter | solution.py:200
  43.1 18.6 %copy-start.3 = (bf16[512,448]{0,1:T(8,128)(2,1)}, bf16[512,448]{0,1:T(8,128)(2,1)S(1)}, u32[]{:S(2)}) copy-start(bf16[512,448]{0,1:T(8,128)(2,1)S(1)} %collective-permute-done) | copy-start | bytes 1376260
  43.1 9.2 %collective-permute-start.1 = (bf16[512,448]{0,1:T(8,128)(2,1)S(1)}, bf16[512,448]{0,1:T(8,128)(2,1)}, u32[]{:S(2)}, u32[]{:S(2)}) collective-permute-start(bf16[512,448]{0,1:T(8,128)(2,1)S(1)} %collective-permute-done), channel_id=1, source_target_pairs={{0,1},{1,2},{2,3},{3,4},{4,5},{5,6},{6,7},{7,0},{8,9},{9,10},{10,1... | collective-permute-start | bytes 1376264 | tf_op jit(solution)/shard_map/ppermute | solution.py:123
  52.3 9.3 %collective-permute-start.2 = (bf16[512,448]{0,1:T(8,128)(2,1)}, bf16[512,448]{0,1:T(8,128)(2,1)S(1)}, u32[]{:S(2)}, u32[]{:S(2)}) collective-permute-start(bf16[512,448]{0,1:T(8,128)(2,1)} %collective-permute-done.1), channel_id=1, source_target_pairs={{0,1},{1,2},{2,3},{3,4},{4,5},{5,6},{6,7},{7,0},{8,9},{9,10},{10,1... | collective-permute-start | bytes 1376264 | tf_op jit(solution)/shard_map/ppermute | solution.py:123
  61.6 9.2 %collective-permute-start.3 = (bf16[512,448]{0,1:T(8,128)(2,1)S(1)}, bf16[512,448]{0,1:T(8,128)(2,1)}, u32[]{:S(2)}, u32[]{:S(2)}) collective-permute-start(bf16[512,448]{0,1:T(8,128)(2,1)S(1)} %collective-permute-done.2), channel_id=1, source_target_pairs={{0,1},{1,2},{2,3},{3,4},{4,5},{5,6},{6,7},{7,0},{8,9},{9,10},{10,1... | collective-permute-start | bytes 1376264 | tf_op jit(solution)/shard_map/ppermute | solution.py:123
  70.9 9.4 %collective-permute-start.4 = (bf16[512,448]{0,1:T(8,128)(2,1)}, bf16[512,448]{0,1:T(8,128)(2,1)}, u32[]{:S(2)}, u32[]{:S(2)}) collective-permute-start(bf16[512,448]{0,1:T(8,128)(2,1)} %collective-permute-done.3), channel_id=1, source_target_pairs={{0,1},{1,2},{2,3},{3,4},{4,5},{5,6},{6,7},{7,0},{8,9},{9,10},{10,1... | collective-permute-start | bytes 1376264 | tf_op jit(solution)/shard_map/ppermute | solution.py:123
  80.3 9.4 %collective-permute-start.5 = (bf16[512,448]{0,1:T(8,128)(2,1)}, bf16[512,448]{0,1:T(8,128)(2,1)}, u32[]{:S(2)}, u32[]{:S(2)}) collective-permute-start(bf16[512,448]{0,1:T(8,128)(2,1)} %collective-permute-done.4), channel_id=1, source_target_pairs={{0,1},{1,2},{2,3},{3,4},{4,5},{5,6},{6,7},{7,0},{8,9},{9,10},{10,1... | collective-permute-start | bytes 1376264 | tf_op jit(solution)/shard_map/ppermute | solution.py:123
  81.8 24.8 %copy-start.2 = (bf16[512,448]{0,1:T(8,128)(2,1)S(1)}, bf16[512,448]{0,1:T(8,128)(2,1)}, u32[]{:S(2)}) copy-start(bf16[512,448]{0,1:T(8,128)(2,1)} %param.16) | copy-start | bytes 1376260
  89.7 9.4 %collective-permute-start.6 = (bf16[512,448]{0,1:T(8,128)(2,1)}, bf16[512,448]{0,1:T(8,128)(2,1)}, u32[]{:S(2)}, u32[]{:S(2)}) collective-permute-start(bf16[512,448]{0,1:T(8,128)(2,1)} %collective-permute-done.5), channel_id=1, source_target_pairs={{0,1},{1,2},{2,3},{3,4},{4,5},{5,6},{6,7},{7,0},{8,9},{9,10},{10,1... | collective-permute-start | bytes 1376264 | tf_op jit(solution)/shard_map/ppermute | solution.py:123
  89.8 21.0 %copy-start.6 = (bf16[512,448]{0,1:T(8,128)(2,1)S(1)}, bf16[512,448]{0,1:T(8,128)(2,1)}, u32[]{:S(2)}) copy-start(bf16[512,448]{0,1:T(8,128)(2,1)} %copy-done.5) | copy-start | bytes 1376260
  89.8 22.1 %copy-start.4 = (bf16[512,448]{0,1:T(8,128)(2,1)S(1)}, bf16[512,448]{0,1:T(8,128)(2,1)}, u32[]{:S(2)}) copy-start(bf16[512,448]{0,1:T(8,128)(2,1)} %copy-done.3) | copy-start | bytes 1376260
  103.4 9.9 %copy-start.10 = (f32[3584]{0:T(1024)S(1)}, f32[3584]{0:T(1024)}, u32[]{:S(2)}) copy-start(f32[3584]{0:T(1024)} %param.17) | copy-start | bytes 43012
  115.1 1.9 copy-start.1
  120.1 53.1 %collective-permute-start.8 = (bf16[512,256]{0,1:T(8,128)(2,1)}, bf16[512,256]{0,1:T(8,128)(2,1)}, u32[]{:S(2)}, u32[]{:S(2)}) collective-permute-start(bf16[512,256]{0,1:T(8,128)(2,1)} %maximum_bitcast_fusion.6), channel_id=1, source_target_pairs={{0,8},{8,16},{16,24},{24,32},{32,40},{40,48},{48,56},{56,64},{64,7... | collective-permute-start | bytes 786440 | tf_op jit(solution)/shard_map/ppermute | solution.py:14
  130.3 44.7 %collective-permute-start.7 = (bf16[512,256]{1,0:T(8,128)(2,1)}, bf16[512,256]{1,0:T(8,128)(2,1)}, u32[]{:S(2)}, u32[]{:S(2)}) collective-permute-start(bf16[512,256]{1,0:T(8,128)(2,1)} %convolution_convert_fusion.1), channel_id=1, source_target_pairs={{0,8},{8,16},{16,24},{24,32},{32,40},{40,48},{48,56},{56,64},{64,7... | collective-permute-start | bytes 786440 | tf_op jit(solution)/shard_map/ppermute | solution.py:14
  191.4 2.2 copy-start.7
  191.4 2.2 copy-start.8
  191.4 2.2 copy-start.9
  193.7 2.8 %copy-start.11 = (bf16[512,3584]{1,0:T(8,128)(2,1)S(1)}, bf16[512,3584]{1,0:T(8,128)(2,1)}, u32[]{:S(2)}) copy-start(bf16[512,3584]{1,0:T(8,128)(2,1)} %param.21) | copy-start | bytes 11010052
  (1 other events, 0.8 us)
Sparse Core Ops, SparseCore 0:
  9.5 45.2 all-gather.7
  56.9 50.9 all-gather.5
  110.1 54.2 all-gather.3
  200.5 34.8 reduce-scatter.1
